TPU v7x, 32 devices: a whole 2x2x4 slice. The times are simulated.
32 devices in a mesh: groups: 2 (over x), gx: 8 (over z, y), gy: 2 (over core).
Axes of the slice: x: 2, y: 2, z: 4, core: 2. Of those that a mesh axis runs over, the one named last changes fastest.
Arguments:
- values: float32 [96, 12, 64, 128], P(('groups', 'gx'), 'gy'), parts along dimension 0, may hold values from -6 to 6
- drift: float32 [2, 96, 12], P(None, ('groups', 'gx'), 'gy'), parts along dimension 1, may hold values from -6 to 6
- params: float32 [8], P('groups'), parts along dimension 0, may hold values from 0.5 to 1.5
Outputs:
- advanced: float32 [96, 12, 64, 128], P(('groups', 'gx'), 'gy'), parts along dimension 0
There are 2 independent parts, one for each index of `groups`. A program takes and returns all parts, laid end to end along the dimension named above; each array names one. Nothing has to cross between parts.
All inputs are finite; a program needn't handle non-finite values.
Results may differ from a plain program's by a relative error of at most 0.0003.
Values sent between devices are 32-bit elements; how exact they have to be, the bound alone decides.
No kernel may reach another device: no remote copies, remote signals or barrier semaphores. Data moves between devices by JAX's collectives and lax.ppermute only.
A program may use at most 64 MiB of HBM per device.

v0:
```python
import math

import jax
import jax.numpy as jnp
from jax import lax
from jax.sharding import PartitionSpec as P

cfl_number = 0.5
weno_eps = 1e-06
cell_span = 1.0 / 64.0


def with_halo(cells, sides, width):
    for axis, dim in sides:
        count = lax.axis_size(axis)
        ends = count - 1
        head = lax.slice_in_dim(cells, 0, width, axis=dim)
        tail = lax.slice_in_dim(cells, cells.shape[dim] - width, cells.shape[dim], axis=dim)
        cells = jnp.concatenate(
            [
                lax.ppermute(tail, axis, [(i, (i + 1) % count) for i in range(ends)]),
                cells,
                lax.ppermute(head, axis, [((i + 1) % count, i) for i in range(ends)]),
            ],
            axis=dim,
        )
    return cells


def weno_value(first, second, third, fourth, fifth):
    stencil_one = first / 3.0 - 7.0 * second / 6.0 + 11.0 * third / 6.0
    stencil_two = -second / 6.0 + 5.0 * third / 6.0 + fourth / 3.0
    stencil_three = third / 3.0 + 5.0 * fourth / 6.0 - fifth / 6.0
    smooth_one = (
        13.0 / 12.0 * (first - 2.0 * second + third) ** 2
        + 0.25 * (first - 4.0 * second + 3.0 * third) ** 2
    )
    smooth_two = 13.0 / 12.0 * (second - 2.0 * third + fourth) ** 2 + 0.25 * (second - fourth) ** 2
    smooth_three = (
        13.0 / 12.0 * (third - 2.0 * fourth + fifth) ** 2
        + 0.25 * (3.0 * third - 4.0 * fourth + fifth) ** 2
    )
    weight_one = 0.1 / (weno_eps + smooth_one) ** 2
    weight_two = 0.6 / (weno_eps + smooth_two) ** 2
    weight_three = 0.3 / (weno_eps + smooth_three) ** 2
    total = weight_one * stencil_one + weight_two * stencil_two + weight_three * stencil_three
    return total / (weight_one + weight_two + weight_three)


def both_sides(window):
    backward = weno_value(window(0), window(1), window(2), window(3), window(4))
    forward = weno_value(window(5), window(4), window(3), window(2), window(1))
    return (backward, forward)


def one_sided(padded, along, spacing, length):
    extent = padded.shape[along]
    differences = (
        lax.slice_in_dim(padded, 1, extent, axis=along)
        - lax.slice_in_dim(padded, 0, extent - 1, axis=along)
    ) / spacing

    def window(offset):
        return lax.slice_in_dim(differences, offset, offset + length, axis=along)

    return both_sides(window)


def periodic_sided(field, along, spacing):
    differences = (field - jnp.roll(field, 1, axis=along)) / spacing

    def window(offset):
        return jnp.roll(differences, 2 - offset, axis=along)

    return both_sides(window)


def clamped_sided(field, along, spacing):
    extent = field.shape[along]
    inner = (
        lax.slice_in_dim(field, 1, extent, axis=along)
        - lax.slice_in_dim(field, 0, extent - 1, axis=along)
    ) / spacing
    differences = jnp.concatenate([lax.slice_in_dim(inner, 0, 1, axis=along), inner], axis=along)
    low_edge = lax.slice_in_dim(differences, 0, 1, axis=along)
    high_edge = lax.slice_in_dim(differences, extent - 1, extent, axis=along)

    def window(offset):
        shift_by = offset - 2
        if shift_by > 0:
            return jnp.concatenate(
                [lax.slice_in_dim(differences, shift_by, extent, axis=along)]
                + [high_edge] * shift_by,
                axis=along,
            )
        if shift_by < 0:
            return jnp.concatenate(
                [low_edge] * -shift_by
                + [lax.slice_in_dim(differences, 0, extent + shift_by, axis=along)],
                axis=along,
            )
        return differences

    return both_sides(window)


def edge_fill(field, along, margin, at_low, at_high):
    extent = field.shape[along]
    shape_dist = [1] * field.ndim
    shape_dist[along] = margin
    inner_low = lax.slice_in_dim(field, margin, margin + 1, axis=along)
    next_low = lax.slice_in_dim(field, margin + 1, margin + 2, axis=along)
    dist_low = jnp.arange(margin, 0, -1).astype(jnp.float32).reshape(tuple(shape_dist))
    low_fill = inner_low + dist_low * (inner_low - next_low)
    inner_high = lax.slice_in_dim(field, extent - margin - 1, extent - margin, axis=along)
    next_high = lax.slice_in_dim(field, extent - margin - 2, extent - margin - 1, axis=along)
    dist_high = jnp.arange(1, margin + 1).astype(jnp.float32).reshape(tuple(shape_dist))
    high_fill = inner_high + dist_high * (inner_high - next_high)
    new_low = jnp.where(at_low, low_fill, lax.slice_in_dim(field, 0, margin, axis=along))
    new_high = jnp.where(
        at_high, high_fill, lax.slice_in_dim(field, extent - margin, extent, axis=along)
    )
    middle = lax.slice_in_dim(field, margin, extent - margin, axis=along)
    return jnp.concatenate([new_low, middle, new_high], axis=along)


def speed_bounds(drift_field, x_coord, y_coord, turn_a, along_one, along_two):
    first_hi = jnp.max(along_one)
    first_lo = jnp.min(along_one)
    second_hi = jnp.max(along_two)
    second_lo = jnp.min(along_two)
    bound_one = jnp.max(
        jnp.maximum(drift_field[0] + first_hi, -(drift_field[0] + first_lo))
        + turn_a * jnp.abs(y_coord)[None, :]
    )
    bound_two = jnp.max(
        jnp.maximum(drift_field[1] + second_hi, -(drift_field[1] + second_lo))
        + turn_a * jnp.abs(x_coord)[:, None]
    )
    return (bound_one, bound_two)


def hamilton_rate(
    backs, fores, x_coord, y_coord, flow_x, flow_y, along_one, along_two, params, alphas
):
    mean_one = 0.5 * (backs[0] + fores[0])
    mean_two = 0.5 * (backs[1] + fores[1])
    mean_three = 0.5 * (backs[2] + fores[2])
    mean_four = 0.5 * (backs[3] + fores[3])
    x_col = x_coord[:, None, None, None]
    y_col = y_coord[None, :, None, None]
    ham = mean_one * (along_one[None, None] + flow_x[:, :, None, None])
    ham = ham + mean_two * (along_two[None, None] + flow_y[:, :, None, None])
    ham = ham + params[1] * jnp.abs(mean_one * y_col - mean_two * x_col - mean_three)
    ham = ham - params[2] * jnp.abs(mean_three) + params[3] * jnp.abs(mean_four)
    dissipation = alphas[0] * (fores[0] - backs[0]) + alphas[1] * (fores[1] - backs[1])
    dissipation = (
        dissipation + alphas[2] * (fores[2] - backs[2]) + alphas[3] * (fores[3] - backs[3])
    )
    return ham + 0.5 * dissipation


def on_device(values, drift, params):
    cells_x, cells_y, n_psi, n_speed = values.shape
    devices_x = lax.axis_size("gx")
    devices_y = lax.axis_size("gy")
    total_x = cells_x * devices_x
    total_y = cells_y * devices_y
    step_psi = 2.0 * math.pi / n_psi
    step_speed = 1.0 / n_speed
    place_x = lax.axis_index("gx")
    place_y = lax.axis_index("gy")
    first_x = place_x == 0
    last_x = place_x == devices_x - 1
    first_y = place_y == 0
    last_y = place_y == devices_y - 1
    psi_grid = jnp.arange(n_psi).astype(jnp.float32) * step_psi - math.pi
    speed_grid = 0.5 + (jnp.arange(n_speed).astype(jnp.float32) + 0.5) * step_speed
    along_one = -speed_grid[None, :] + params[0] * jnp.cos(psi_grid)[:, None]
    along_two = params[0] * jnp.sin(psi_grid)[:, None]
    y_coord = (
        (place_y * cells_y + jnp.arange(cells_y)).astype(jnp.float32) + 0.5 - 0.5 * total_y
    ) * cell_span
    x_local = (
        (place_x * cells_x + jnp.arange(cells_x)).astype(jnp.float32) + 0.5 - 0.5 * total_x
    ) * cell_span
    local_one, local_two = speed_bounds(drift, x_local, y_coord, params[1], along_one, along_two)
    bound_one, bound_two = lax.pmax((local_one, local_two), ("gx", "gy"))
    alphas = (bound_one, bound_two, params[1] + params[2], params[3])
    step_time = cfl_number / (
        alphas[0] / cell_span
        + alphas[1] / cell_span
        + alphas[2] / step_psi
        + alphas[3] / step_speed
    )

    def section_rate(extended, margin, drift_wide):
        filled = edge_fill(extended, 0, margin, first_x, last_x)
        width = filled.shape[0] - 6
        back_one, fore_one = one_sided(filled, 0, cell_span, width)
        core = filled[3 : 3 + width]
        wide_y = with_halo(core, (("gy", 1),), 3)
        wide_y = edge_fill(wide_y, 1, 3, first_y, last_y)
        back_two, fore_two = one_sided(wide_y, 1, cell_span, cells_y)
        back_three, fore_three = periodic_sided(core, 2, step_psi)
        back_four, fore_four = clamped_sided(core, 3, step_speed)
        x_coord = (
            (place_x * cells_x - (margin - 3) + jnp.arange(width)).astype(jnp.float32)
            + 0.5
            - 0.5 * total_x
        ) * cell_span
        return hamilton_rate(
            (back_one, back_two, back_three, back_four),
            (fore_one, fore_two, fore_three, fore_four),
            x_coord,
            y_coord,
            drift_wide[0],
            drift_wide[1],
            along_one,
            along_two,
            params,
            alphas,
        )

    def with_rim(field):
        return with_halo(field, (("gx", 0),), 3)

    first = values + step_time * section_rate(with_rim(values), 3, drift)
    second = 0.75 * values + 0.25 * (first + step_time * section_rate(with_rim(first), 3, drift))
    result = values * (1.0 / 3.0) + 2.0 / 3.0 * (
        second + step_time * section_rate(with_rim(second), 3, drift)
    )
    return result


def solution(mesh):
    in_specs = (P(("groups", "gx"), "gy", None, None), P(None, ("groups", "gx"), "gy"), P("groups"))
    out_specs = P(("groups", "gx"), "gy", None, None)
    return jax.shard_map(
        on_device, mesh=mesh, in_specs=in_specs, out_specs=out_specs, check_vma=False
    )
```

profile of v0, /device:TPU:0, one launch (start us, length us, event | category | flops | bytes accessed | tf_op | source)
XLA Modules:
  0.0 234.5 jit_solution(4289693595073107375)
XLA Ops:
  0.0 2.5 %fusion.62 = (f32[3,6,64,128]{3,2,1,0:T(8,128)}, f32[3,6,64,128]{3,2,1,0:T(8,128)}) fusion(f32[6,6,64,128]{3,2,1,0:T(8,128)} %param.3), kind=kLoop, calls=%fused_computation.173 | loop fusion | bytes 2359296 | tf_op jit(solution)/shard_map/slice | solution.py:18
  2.5 1.3 collective-permute-start.1
  3.8 6.4 %collective-permute-start = (f32[3,6,64,128]{3,2,1,0:T(8,128)}, f32[3,6,64,128]{3,2,1,0:T(8,128)}, u32[]{:S(2)}, u32[]{:S(2)}) collective-permute-start(f32[3,6,64,128]{3,2,1,0:T(8,128)} %get-tuple-element.61), channel_id=1, source_target_pairs={{0,2},{2,4},{4,6},{6,8},{8,10},{10,12},{12,14},{1,3},{3,5},{5,7},{... | collective-permute-start | bytes 1769480 | tf_op jit(solution)/shard_map/ppermute | solution.py:21
  10.2 1.1 fusion.63
  11.3 1.3 collective-permute-start.3
  12.6 4.7 %collective-permute-start.2 = (f32[6,3,64,128]{3,2,1,0:T(8,128)}, f32[6,3,64,128]{3,2,1,0:T(8,128)}, u32[]{:S(2)}, u32[]{:S(2)}) collective-permute-start(f32[6,3,64,128]{3,2,1,0:T(8,128)} %get-tuple-element.67), channel_id=1, source_target_pairs={{0,1},{2,3},{4,5},{6,7},{8,9},{10,11},{12,13},{14,15},{16,17},{18,... | collective-permute-start | bytes 1769480 | tf_op jit(solution)/shard_map/ppermute | solution.py:21
  17.3 0.5 add_negate_fusion
  17.8 0.7 fusion.70
  18.5 1.8 cosine_multiply_fusion
  20.3 1.4 fusion.47
  21.7 0.9 slice_bitcast_fusion.11
  22.6 0.9 slice_bitcast_fusion.9
  23.6 0.4 subtract_multiply_fusion
  23.9 1.2 sine_multiply_fusion
  25.2 0.6 copy-done.22
  26.2 1.6 fusion.65
  27.7 0.6 fusion.66
  28.4 0.6 fusion.64
  29.0 0.6 fusion.44
  29.6 0.6 abs_multiply_fusion
  30.2 1.4 fusion.68
  31.7 2.1 slice_maximum_fusion.5
  33.8 1.3 add_reduce_fusion.1
  35.2 0.7 add_multiply_fusion.3
  35.9 1.9 add_reduce_fusion.2
  37.8 1.9 add_reduce_fusion.3
  39.7 1.4 slice_maximum_fusion.4
  41.2 31.2 %all-reduce = (f32[]{:T(128)}, f32[]{:T(128)}) all-reduce(f32[]{:T(128)} %add_reduce_fusion.2, f32[]{:T(128)} %add_reduce_fusion.3), channel_id=1, replica_groups=mesh['groups'=2,'gx'=8,'gy'=2] {'gx','gy'}, use_global_device_ids=true, to_apply=%region_7.0 | all-reduce | flops 2 | bytes 16 | tf_op jit(solution)/shard_map/pmax | solution.py:188
  72.4 1.2 slice.701
  73.6 0.6 slice.702
  74.2 1.4 slice.710
  79.2 0.6 copy-done.17
  79.9 1.2 add_select_fusion.10
  81.6 0.6 copy-done.13
  82.3 1.2 add_select_fusion.8
  83.5 0.4 fusion.5
  84.0 0.5 copy-done.11
  85.2 0.4 fusion.4
  87.0 0.4 copy-done.2
  88.9 27.5 %fusion.12 = f32[6,6,64,128]{3,2,1,0:T(8,128)S(1)} fusion(f32[6,6,64,128]{3,2,1,0:T(8,128)S(1)} %copy-done, f32[6,6,64,1]{3,2,1,0:T(8,128)S(1)} %copy-done.8, f32[6,6,64,125]{3,2,1,0:T(8,128)S(1)} %copy-done.5, f32[6,6,64,126]{3,2,1,0:T(8,128)S(1)} %copy-done.10, f32[6,6,64,127]{3,2,1,0:T(8,128)S(1)} %subtract_multiply_fusion, ...), kind=kLoop, calls=%fused_computation.27 | loop fusion | flops 163086336 | bytes 29468892 | tf_op jit(solution)/shard_map/add | solution.py:228
  117.8 0.4 fusion.32
  118.2 1.3 collective-permute-start.4
  119.6 1.3 collective-permute-start.5
  120.9 1.3 collective-permute-start.7
  122.2 0.4 fusion.61
  122.6 0.4 slice_maximum_fusion.2
  123.4 3.3 %collective-permute-start.6 = (f32[6,3,64,128]{3,2,1,0:T(8,128)S(1)}, f32[6,3,64,128]{3,2,1,0:T(8,128)S(1)}, u32[]{:S(2)}, u32[]{:S(2)}) collective-permute-start(f32[6,3,64,128]{3,2,1,0:T(8,128)S(1)} %get-tuple-element.43), channel_id=1, source_target_pairs={{0,1},{2,3},{4,5},{6,7},{8,9},{10,11},{12,13},{14,15},{16,17},{18,... | collective-permute-start | bytes 1769480 | tf_op jit(solution)/shard_map/ppermute | solution.py:21
  126.6 0.7 slice_maximum_fusion.3
  127.3 16.6 %collective-permute-done.4 = f32[3,6,64,128]{3,2,1,0:T(8,128)S(1)} collective-permute-done((f32[3,6,64,128]{3,2,1,0:T(8,128)S(1)}, f32[3,6,64,128]{3,2,1,0:T(8,128)S(1)}, u32[]{:S(2)}, u32[]{:S(2)}) %collective-permute-start.4) | collective-permute-done | bytes 589856 | tf_op jit(solution)/shard_map/ppermute | solution.py:21
  144.7 0.4 fusion.3
  145.5 0.4 fusion.2
  146.0 27.7 %fusion.21 = f32[6,6,64,128]{3,2,1,0:T(8,128)S(1)} fusion(f32[6,6,64,128]{3,2,1,0:T(8,128)S(1)} %fusion.12, f32[6,6,64,1]{3,2,1,0:T(8,128)S(1)} %get-tuple-element.56, f32[6,6,64,125]{3,2,1,0:T(8,128)S(1)} %slice.760, f32[6,6,64,126]{3,2,1,0:T(8,128)S(1)} %get-tuple-element.54, f32[6,6,64,127]{3,2,1,0:T(8,128)S(1)} %fusion.32, ...), kind=kLoop, calls=%fused_computation.36 | loop fusion | flops 163971072 | bytes 30648540 | tf_op jit(solution)/shard_map/add | solution.py:229
  175.1 0.4 fusion.31
  175.5 4.4 %collective-permute-start.8 = (f32[3,6,64,128]{3,2,1,0:T(8,128)S(1)}, f32[3,6,64,128]{3,2,1,0:T(8,128)S(1)}, u32[]{:S(2)}, u32[]{:S(2)}) collective-permute-start(f32[3,6,64,128]{3,2,1,0:T(8,128)S(1)} %get-tuple-element.13), channel_id=1, source_target_pairs={{0,2},{2,4},{4,6},{6,8},{8,10},{10,12},{12,14},{1,3},{3,5},{5,7},{... | collective-permute-start | bytes 1769480 | tf_op jit(solution)/shard_map/ppermute | solution.py:21
  180.0 1.3 collective-permute-start.9
  181.3 1.3 collective-permute-start.11
  182.6 0.4 fusion.54
  183.0 0.4 slice_maximum_fusion
  183.8 3.1 %collective-permute-start.10 = (f32[6,3,64,128]{3,2,1,0:T(8,128)S(1)}, f32[6,3,64,128]{3,2,1,0:T(8,128)S(1)}, u32[]{:S(2)}, u32[]{:S(2)}) collective-permute-start(f32[6,3,64,128]{3,2,1,0:T(8,128)S(1)} %get-tuple-element.19), channel_id=1, source_target_pairs={{0,1},{2,3},{4,5},{6,7},{8,9},{10,11},{12,13},{14,15},{16,17},{18,... | collective-permute-start | bytes 1769480 | tf_op jit(solution)/shard_map/ppermute | solution.py:21
  186.9 0.7 slice_maximum_fusion.1
  187.5 16.5 %collective-permute-done.8 = f32[3,6,64,128]{3,2,1,0:T(8,128)S(1)} collective-permute-done((f32[3,6,64,128]{3,2,1,0:T(8,128)S(1)}, f32[3,6,64,128]{3,2,1,0:T(8,128)S(1)}, u32[]{:S(2)}, u32[]{:S(2)}) %collective-permute-start.8) | collective-permute-done | bytes 589856 | tf_op jit(solution)/shard_map/ppermute | solution.py:21
  204.8 0.4 fusion.1
  205.7 0.4 fusion
  206.1 28.4 %fusion.30 = f32[6,6,64,128]{3,2,1,0:T(8,128)} fusion(f32[6,6,64,128]{3,2,1,0:T(8,128)S(1)} %fusion.21, f32[6,6,64,1]{3,2,1,0:T(8,128)S(1)} %get-tuple-element.32, f32[6,6,64,125]{3,2,1,0:T(8,128)S(1)} %slice.810, f32[6,6,64,126]{3,2,1,0:T(8,128)S(1)} %get-tuple-element.30, f32[6,6,64,127]{3,2,1,0:T(8,128)S(1)} %fusion.31, ...), kind=kLoop, calls=%fused_computation.45 | loop fusion | flops 163971072 | bytes 30648540 | tf_op jit(solution)/shard_map/add | solution.py:230
  (125 shorter events, 10.5 us)
Async XLA Ops:
  0.0 10.2 %copy-start = (f32[6,6,64,128]{3,2,1,0:T(8,128)S(1)}, f32[6,6,64,128]{3,2,1,0:T(8,128)}, u32[]{:S(2)}) copy-start(f32[6,6,64,128]{3,2,1,0:T(8,128)} %param.3) | copy-start | bytes 3538948
  2.5 76.7 %collective-permute-start.1 = (f32[3,6,64,128]{3,2,1,0:T(8,128)}, f32[3,6,64,128]{3,2,1,0:T(8,128)}, u32[]{:S(2)}, u32[]{:S(2)}) collective-permute-start(f32[3,6,64,128]{3,2,1,0:T(8,128)} %get-tuple-element.62), channel_id=1, source_target_pairs={{2,0},{4,2},{6,4},{8,6},{10,8},{12,10},{14,12},{3,1},{5,3},{7,5},{... | collective-permute-start | bytes 1769480 | tf_op jit(solution)/shard_map/ppermute | solution.py:23
  3.8 14.0 %copy-start.30 = (f32[4]{0:T(128)S(1)}, f32[4]{0:T(128)}, u32[]{:S(2)}) copy-start(f32[4]{0:T(128)} %param.5) | copy-start | bytes 52
  3.8 77.3 %collective-permute-start = (f32[3,6,64,128]{3,2,1,0:T(8,128)}, f32[3,6,64,128]{3,2,1,0:T(8,128)}, u32[]{:S(2)}, u32[]{:S(2)}) collective-permute-start(f32[3,6,64,128]{3,2,1,0:T(8,128)} %get-tuple-element.61), channel_id=1, source_target_pairs={{0,2},{2,4},{4,6},{6,8},{8,10},{10,12},{12,14},{1,3},{3,5},{5,7},{... | collective-permute-start | bytes 1769480 | tf_op jit(solution)/shard_map/ppermute | solution.py:21
  11.3 70.3 %collective-permute-start.3 = (f32[6,3,64,128]{3,2,1,0:T(8,128)}, f32[6,3,64,128]{3,2,1,0:T(8,128)}, u32[]{:S(2)}, u32[]{:S(2)}) collective-permute-start(f32[6,3,64,128]{3,2,1,0:T(8,128)} %get-tuple-element.68), channel_id=1, source_target_pairs={{1,0},{3,2},{5,4},{7,6},{9,8},{11,10},{13,12},{15,14},{17,16},{19,... | collective-permute-start | bytes 1769480 | tf_op jit(solution)/shard_map/ppermute | solution.py:23
  12.6 71.4 %collective-permute-start.2 = (f32[6,3,64,128]{3,2,1,0:T(8,128)}, f32[6,3,64,128]{3,2,1,0:T(8,128)}, u32[]{:S(2)}, u32[]{:S(2)}) collective-permute-start(f32[6,3,64,128]{3,2,1,0:T(8,128)} %get-tuple-element.67), channel_id=1, source_target_pairs={{0,1},{2,3},{4,5},{6,7},{8,9},{10,11},{12,13},{14,15},{16,17},{18,... | collective-permute-start | bytes 1769480 | tf_op jit(solution)/shard_map/ppermute | solution.py:21
  25.2 0.6 copy-start.22
  26.1 4.1 %copy-start.31 = (f32[2,6,6]{2,0,1:T(2,128)S(1)}, f32[2,6,6]{2,0,1:T(2,128)}, u32[]{:S(2)}) copy-start(f32[2,6,6]{2,0,1:T(2,128)} %param.4) | copy-start | bytes 868
  31.7 8.0 %copy-start.1 = (f32[6,6,64,1]{3,2,1,0:T(8,128)}, f32[6,6,64,1]{3,2,1,0:T(8,128)S(1)}, u32[]{:S(2)}) copy-start(f32[6,6,64,1]{3,2,1,0:T(8,128)S(1)} %get-tuple-element.79) | copy-start | bytes 27652
  31.7 2.1 copy-start.32
  31.7 2.1 copy-start.33
  31.7 3.5 %copy-start.34 = (f32[64]{0:T(128)S(1)}, f32[64]{0:T(128)}, u32[]{:S(2)}) copy-start(f32[64]{0:T(128)} %sine_multiply_fusion) | copy-start | bytes 772
  78.8 0.9 copy-start.17
  78.9 1.0 copy-start.18
  79.1 2.0 copy-start.15
  79.1 2.0 copy-start.16
  81.3 0.9 copy-start.13
  81.3 1.0 copy-start.14
  83.5 0.9 copy-start.11
  83.5 1.0 copy-start.12
  84.7 1.3 copy-start.7
  84.7 1.6 copy-start.8
  84.7 2.0 copy-start.9
  84.7 2.3 copy-start.10
  85.0 2.4 %copy-start.2 = (f32[6,6,64,1]{3,2,1,0:T(8,128)S(1)}, f32[6,6,64,1]{3,2,1,0:T(8,128)}, u32[]{:S(2)}) copy-start(f32[6,6,64,1]{3,2,1,0:T(8,128)} %copy-done.1) | copy-start | bytes 27652
  85.0 2.8 %copy-start.3 = (f32[6,6,64,127]{3,2,1,0:T(8,128)S(1)}, f32[6,6,64,127]{3,2,1,0:T(8,128)}, u32[]{:S(2)}) copy-start(f32[6,6,64,127]{3,2,1,0:T(8,128)} %slice_maximum_fusion.4) | copy-start | bytes 3511300
  85.0 3.1 %copy-start.4 = (f32[6,6,61,128]{3,2,1,0:T(8,128)S(1)}, f32[6,6,61,128]{3,2,1,0:T(8,128)}, u32[]{:S(2)}) copy-start(f32[6,6,61,128]{3,2,1,0:T(8,128)} %slice.701) | copy-start | bytes 3373060
  85.1 3.4 %copy-start.5 = (f32[6,6,64,125]{3,2,1,0:T(8,128)S(1)}, f32[6,6,64,125]{3,2,1,0:T(8,128)}, u32[]{:S(2)}) copy-start(f32[6,6,64,125]{3,2,1,0:T(8,128)} %slice.710) | copy-start | bytes 3456004
  85.1 3.8 %copy-start.6 = (f32[6,6,63,128]{3,2,1,0:T(8,128)S(1)}, f32[6,6,63,128]{3,2,1,0:T(8,128)}, u32[]{:S(2)}) copy-start(f32[6,6,63,128]{3,2,1,0:T(8,128)} %get-tuple-element.71) | copy-start | bytes 3483652
  85.1 3.8 %copy-start.19 = (f32[64,128]{1,0:T(8,128)S(1)}, f32[64,128]{1,0:T(8,128)}, u32[]{:S(2)}) copy-start(f32[64,128]{1,0:T(8,128)} %get-tuple-element.83) | copy-start | bytes 98308
  85.1 3.8 %copy-start.20 = (f32[6,6,64]{2,1,0:T(8,128)S(1)}, f32[6,6,64]{2,1,0:T(8,128)}, u32[]{:S(2)}) copy-start(f32[6,6,64]{2,1,0:T(8,128)} %add_multiply_fusion.3) | copy-start | bytes 27652
  85.1 3.7 %copy-start.21 = (f32[6,6,3,128]{3,2,1,0:T(4,128)S(1)}, f32[6,6,3,128]{3,2,1,0:T(4,128)}, u32[]{:S(2)}) copy-start(f32[6,6,3,128]{3,2,1,0:T(4,128)} %slice.702) | copy-start | bytes 165892
  85.1 3.7 %copy-start.23 = (f32[6,6,1,128]{3,2,1,0:T(1,128)S(1)}, f32[6,6,1,128]{3,2,1,0:T(1,128)}, u32[]{:S(2)}) copy-start(f32[6,6,1,128]{3,2,1,0:T(1,128)} %copy-done.22) | copy-start | bytes 55300
  85.1 3.7 %copy-start.24 = (f32[6,6,2,128]{3,2,1,0:T(2,128)S(1)}, f32[6,6,2,128]{3,2,1,0:T(2,128)}, u32[]{:S(2)}) copy-start(f32[6,6,2,128]{3,2,1,0:T(2,128)} %get-tuple-element.73) | copy-start | bytes 110596
  85.1 3.7 %copy-start.25 = (f32[6,6,2,128]{3,2,1,0:T(2,128)S(1)}, f32[6,6,2,128]{3,2,1,0:T(2,128)}, u32[]{:S(2)}) copy-start(f32[6,6,2,128]{3,2,1,0:T(2,128)} %get-tuple-element.74) | copy-start | bytes 110596
  85.1 3.7 %copy-start.26 = (f32[6,6,1,128]{3,2,1,0:T(1,128)S(1)}, f32[6,6,1,128]{3,2,1,0:T(1,128)}, u32[]{:S(2)}) copy-start(f32[6,6,1,128]{3,2,1,0:T(1,128)} %get-tuple-element.69) | copy-start | bytes 55300
  85.1 3.7 %copy-start.27 = (f32[6,6,1,128]{3,2,1,0:T(1,128)S(1)}, f32[6,6,1,128]{3,2,1,0:T(1,128)}, u32[]{:S(2)}) copy-start(f32[6,6,1,128]{3,2,1,0:T(1,128)} %get-tuple-element.70) | copy-start | bytes 55300
  85.2 3.7 %copy-start.28 = (f32[6]{0:T(128)S(1)}, f32[6]{0:T(128)}, u32[]{:S(2)}) copy-start(f32[6]{0:T(128)} %get-tuple-element.92) | copy-start | bytes 76
  85.2 3.7 %copy-start.29 = (f32[6]{0:T(128)S(1)}, f32[6]{0:T(128)}, u32[]{:S(2)}) copy-start(f32[6]{0:T(128)} %get-tuple-element.93) | copy-start | bytes 76
  118.2 25.7 %collective-permute-start.4 = (f32[3,6,64,128]{3,2,1,0:T(8,128)S(1)}, f32[3,6,64,128]{3,2,1,0:T(8,128)S(1)}, u32[]{:S(2)}, u32[]{:S(2)}) collective-permute-start(f32[3,6,64,128]{3,2,1,0:T(8,128)S(1)} %get-tuple-element.37), channel_id=1, source_target_pairs={{0,2},{2,4},{4,6},{6,8},{8,10},{10,12},{12,14},{1,3},{3,5},{5,7},{... | collective-permute-start | bytes 1769480 | tf_op jit(solution)/shard_map/ppermute | solution.py:21
  119.6 24.5 %collective-permute-start.5 = (f32[3,6,64,128]{3,2,1,0:T(8,128)S(1)}, f32[3,6,64,128]{3,2,1,0:T(8,128)S(1)}, u32[]{:S(2)}, u32[]{:S(2)}) collective-permute-start(f32[3,6,64,128]{3,2,1,0:T(8,128)S(1)} %get-tuple-element.38), channel_id=1, source_target_pairs={{2,0},{4,2},{6,4},{8,6},{10,8},{12,10},{14,12},{3,1},{5,3},{7,5},{... | collective-permute-start | bytes 1769480 | tf_op jit(solution)/shard_map/ppermute | solution.py:23
  120.9 24.2 %collective-permute-start.7 = (f32[6,3,64,128]{3,2,1,0:T(8,128)S(1)}, f32[6,3,64,128]{3,2,1,0:T(8,128)S(1)}, u32[]{:S(2)}, u32[]{:S(2)}) collective-permute-start(f32[6,3,64,128]{3,2,1,0:T(8,128)S(1)} %get-tuple-element.44), channel_id=1, source_target_pairs={{1,0},{3,2},{5,4},{7,6},{9,8},{11,10},{13,12},{15,14},{17,16},{19,... | collective-permute-start | bytes 1769480 | tf_op jit(solution)/shard_map/ppermute | solution.py:23
  123.4 21.1 %collective-permute-start.6 = (f32[6,3,64,128]{3,2,1,0:T(8,128)S(1)}, f32[6,3,64,128]{3,2,1,0:T(8,128)S(1)}, u32[]{:S(2)}, u32[]{:S(2)}) collective-permute-start(f32[6,3,64,128]{3,2,1,0:T(8,128)S(1)} %get-tuple-element.43), channel_id=1, source_target_pairs={{0,1},{2,3},{4,5},{6,7},{8,9},{10,11},{12,13},{14,15},{16,17},{18,... | collective-permute-start | bytes 1769480 | tf_op jit(solution)/shard_map/ppermute | solution.py:21
  175.5 28.5 %collective-permute-start.8 = (f32[3,6,64,128]{3,2,1,0:T(8,128)S(1)}, f32[3,6,64,128]{3,2,1,0:T(8,128)S(1)}, u32[]{:S(2)}, u32[]{:S(2)}) collective-permute-start(f32[3,6,64,128]{3,2,1,0:T(8,128)S(1)} %get-tuple-element.13), channel_id=1, source_target_pairs={{0,2},{2,4},{4,6},{6,8},{8,10},{10,12},{12,14},{1,3},{3,5},{5,7},{... | collective-permute-start | bytes 1769480 | tf_op jit(solution)/shard_map/ppermute | solution.py:21
  180.0 24.2 %collective-permute-start.9 = (f32[3,6,64,128]{3,2,1,0:T(8,128)S(1)}, f32[3,6,64,128]{3,2,1,0:T(8,128)S(1)}, u32[]{:S(2)}, u32[]{:S(2)}) collective-permute-start(f32[3,6,64,128]{3,2,1,0:T(8,128)S(1)} %get-tuple-element.14), channel_id=1, source_target_pairs={{2,0},{4,2},{6,4},{8,6},{10,8},{12,10},{14,12},{3,1},{5,3},{7,5},{... | collective-permute-start | bytes 1769480 | tf_op jit(solution)/shard_map/ppermute | solution.py:23
  181.3 24.0 %collective-permute-start.11 = (f32[6,3,64,128]{3,2,1,0:T(8,128)S(1)}, f32[6,3,64,128]{3,2,1,0:T(8,128)S(1)}, u32[]{:S(2)}, u32[]{:S(2)}) collective-permute-start(f32[6,3,64,128]{3,2,1,0:T(8,128)S(1)} %get-tuple-element.20), channel_id=1, source_target_pairs={{1,0},{3,2},{5,4},{7,6},{9,8},{11,10},{13,12},{15,14},{17,16},{19,... | collective-permute-start | bytes 1769480 | tf_op jit(solution)/shard_map/ppermute | solution.py:23
  183.8 20.9 %collective-permute-start.10 = (f32[6,3,64,128]{3,2,1,0:T(8,128)S(1)}, f32[6,3,64,128]{3,2,1,0:T(8,128)S(1)}, u32[]{:S(2)}, u32[]{:S(2)}) collective-permute-start(f32[6,3,64,128]{3,2,1,0:T(8,128)S(1)} %get-tuple-element.19), channel_id=1, source_target_pairs={{0,1},{2,3},{4,5},{6,7},{8,9},{10,11},{12,13},{14,15},{16,17},{18,... | collective-permute-start | bytes 1769480 | tf_op jit(solution)/shard_map/ppermute | solution.py:21
where the time goes:
time: 235 us
  other arithmetic  114 us (49%)
  waiting for transfers between devices  33.1 us (14%)
  blocking collectives  31.2 us (13%)
  starting transfers between devices  30.9 us (13%)
  local copies, waits for them, and re-layouts  21.5 us (9%)
  between operations  4.23 us (2%)
    ppermute x6, waiting for transfers between devices, with_halo(): lax.ppermute(tail, axis, [(i, (i + 1) % count) for i in range(ends)])  33.1 us
    pmax x1, blocking collectives, on_device(): bound_one, bound_two = lax.pmax((local_one, local_two), ('gx', 'gy'))  31.2 us
    add x1, other arithmetic, on_device(): values * (1.0 / 3.0)  28.4 us
    add x1, other arithmetic, on_device(): 0.75 * values  27.7 us
    add x1, other arithmetic, on_device(): first = values + step_time * section_rate(with_rim(values), 3, drift)  27.5 us
    ppermute x6, starting transfers between devices, with_halo(): lax.ppermute(tail, axis, [(i, (i + 1) % count) for i in range(ends)])  23.2 us
    ppermute x6, starting transfers between devices, with_halo(): lax.ppermute(head, axis, [((i + 1) % count, i) for i in range(ends)])  7.73 us
    slice x18, local copies, waits for them, and re-layouts, window(): return jnp.roll(differences, 2 - offset, axis=along)  6.43 us
  transfers between devices with their start and end apart: 12, of which 2 were waited for; matrix products, arithmetic and copies ran while one was open for 16% of the time, Pallas kernels for 0%

commit v1 on v0

--- a/solution.py
+++ b/solution.py
@@ -158,6 +158,40 @@
         dissipation + alphas[2] * (fores[2] - backs[2]) + alphas[3] * (fores[3] - backs[3])
     )
     return ham + 0.5 * dissipation
+
+
+def exchange(field, width):
+    pieces = []
+    for axis, dim in (("gx", 0), ("gy", 1)):
+        extent = field.shape[dim]
+        pieces.append(lax.slice_in_dim(field, extent - width, extent, axis=dim))
+        pieces.append(lax.slice_in_dim(field, 0, width, axis=dim))
+    *pieces, field = lax.optimization_barrier((*pieces, field))
+    moved = []
+    for index, (axis, dim) in enumerate((("gx", 0), ("gy", 1))):
+        count = lax.axis_size(axis)
+        ends = count - 1
+        tail, head = pieces[2 * index], pieces[2 * index + 1]
+        moved.append(lax.ppermute(tail, axis, [(i, (i + 1) % count) for i in range(ends)]))
+        moved.append(lax.ppermute(head, axis, [((i + 1) % count, i) for i in range(ends)]))
+    return moved, field
+
+
+def spread_max(local, axes):
+    count = 1
+    for axis in axes:
+        count *= lax.axis_size(axis)
+    span = 1
+    while span < count:
+        moved = [
+            lax.ppermute(local, axes, [(i, (i + k * span) % count) for i in range(count)])
+            for k in range(1, 4)
+            if k * span < count
+        ]
+        for item in moved:
+            local = jnp.maximum(local, item)
+        span *= 4
+    return local
 
 
 def on_device(values, drift, params):
@@ -181,55 +215,61 @@
     y_coord = (
         (place_y * cells_y + jnp.arange(cells_y)).astype(jnp.float32) + 0.5 - 0.5 * total_y
     ) * cell_span
-    x_local = (
+    x_coord = (
         (place_x * cells_x + jnp.arange(cells_x)).astype(jnp.float32) + 0.5 - 0.5 * total_x
     ) * cell_span
-    local_one, local_two = speed_bounds(drift, x_local, y_coord, params[1], along_one, along_two)
-    bound_one, bound_two = lax.pmax((local_one, local_two), ("gx", "gy"))
-    alphas = (bound_one, bound_two, params[1] + params[2], params[3])
+    local_one, local_two = speed_bounds(drift, x_coord, y_coord, params[1], along_one, along_two)
+    bounds = spread_max(jnp.stack([local_one, local_two]), ("gx", "gy"))
+    bound_one = bounds[0]
+    bound_two = bounds[1]
+    alpha_three = params[1] + params[2]
+    alpha_four = params[3]
     step_time = cfl_number / (
-        alphas[0] / cell_span
-        + alphas[1] / cell_span
-        + alphas[2] / step_psi
-        + alphas[3] / step_speed
-    )
-
-    def section_rate(extended, margin, drift_wide):
-        filled = edge_fill(extended, 0, margin, first_x, last_x)
-        width = filled.shape[0] - 6
-        back_one, fore_one = one_sided(filled, 0, cell_span, width)
-        core = filled[3 : 3 + width]
-        wide_y = with_halo(core, (("gy", 1),), 3)
-        wide_y = edge_fill(wide_y, 1, 3, first_y, last_y)
+        bound_one / cell_span
+        + bound_two / cell_span
+        + alpha_three / step_psi
+        + alpha_four / step_speed
+    )
+    x_col = x_coord[:, None, None, None]
+    y_col = y_coord[None, :, None, None]
+    flow_x = drift[0][:, :, None, None]
+    flow_y = drift[1][:, :, None, None]
+
+    def local_part(field):
+        back_three, fore_three = periodic_sided(field, 2, step_psi)
+        back_four, fore_four = clamped_sided(field, 3, step_speed)
+        mean_three = 0.5 * (back_three + fore_three)
+        mean_four = 0.5 * (back_four + fore_four)
+        partial = -params[2] * jnp.abs(mean_three) + params[3] * jnp.abs(mean_four)
+        partial = partial + 0.5 * (
+            alpha_three * (fore_three - back_three) + alpha_four * (fore_four - back_four)
+        )
+        return lax.optimization_barrier((mean_three, partial))
+
+    def section_parts(field):
+        (low_x, high_x, low_y, high_y), field = exchange(field, 3)
+        mean_three, partial = local_part(field)
+        wide_x = edge_fill(jnp.concatenate([low_x, field, high_x], axis=0), 0, 3, first_x, last_x)
+        back_one, fore_one = one_sided(wide_x, 0, cell_span, cells_x)
+        wide_y = edge_fill(jnp.concatenate([low_y, field, high_y], axis=1), 1, 3, first_y, last_y)
         back_two, fore_two = one_sided(wide_y, 1, cell_span, cells_y)
-        back_three, fore_three = periodic_sided(core, 2, step_psi)
-        back_four, fore_four = clamped_sided(core, 3, step_speed)
-        x_coord = (
-            (place_x * cells_x - (margin - 3) + jnp.arange(width)).astype(jnp.float32)
-            + 0.5
-            - 0.5 * total_x
-        ) * cell_span
-        return hamilton_rate(
-            (back_one, back_two, back_three, back_four),
-            (fore_one, fore_two, fore_three, fore_four),
-            x_coord,
-            y_coord,
-            drift_wide[0],
-            drift_wide[1],
-            along_one,
-            along_two,
-            params,
-            alphas,
-        )
-
-    def with_rim(field):
-        return with_halo(field, (("gx", 0),), 3)
-
-    first = values + step_time * section_rate(with_rim(values), 3, drift)
-    second = 0.75 * values + 0.25 * (first + step_time * section_rate(with_rim(first), 3, drift))
-    result = values * (1.0 / 3.0) + 2.0 / 3.0 * (
-        second + step_time * section_rate(with_rim(second), 3, drift)
-    )
+        mean_one = 0.5 * (back_one + fore_one)
+        mean_two = 0.5 * (back_two + fore_two)
+        ham = mean_one * (along_one[None, None] + flow_x)
+        ham = ham + mean_two * (along_two[None, None] + flow_y)
+        ham = ham + params[1] * jnp.abs(mean_one * y_col - mean_two * x_col - mean_three)
+        return ham + partial, fore_one - back_one, fore_two - back_two
+
+    def combine(ham, spread_one, spread_two):
+        return ham + 0.5 * (bound_one * spread_one + bound_two * spread_two)
+
+    def section_rate(field):
+        return combine(*section_parts(field))
+
+    early = lax.optimization_barrier(section_parts(values))
+    first = values + step_time * combine(*early)
+    second = 0.75 * values + 0.25 * (first + step_time * section_rate(first))
+    result = values * (1.0 / 3.0) + 2.0 / 3.0 * (second + step_time * section_rate(second))
     return result
 
 

time: 235 us -> 239 us (1.017)
  blocking collectives: 31.2 us -> 0 us
  waiting for transfers between devices: 33.1 us -> 56.6 us
  starting transfers between devices: 30.9 us -> 46.4 us
  local copies, waits for them, and re-layouts: 21.5 us -> 16.5 us
    pmax x1 -> x0, blocking collectives: 31.2 us -> none  [on_device(): bound_one, bound_two = lax.pmax((local_one, local_two), ('gx', 'gy'))]
    ppermute x12 -> x18, waiting for transfers between devices: 33.1 us -> 56.6 us  [the longest x6 24.4 us: exchange(): lax.ppermute(tail, axis, [(i, (i + 1) % count) for i in range(ends)])]
    ppermute x12 -> x18, starting transfers between devices: 30.9 us -> 46.4 us  [the longest x6 28.4 us: exchange(): lax.ppermute(tail, axis, [(i, (i + 1) % count) for i in range(ends)])]
    add x1, other arithmetic: 28.4 us -> 14 us  [on_device(): values * (1.0 / 3.0)]
    sub x0 -> x1, other arithmetic: none -> 10.2 us  [section_parts(): return (ham + partial, fore_one - back_one, fore_two - back_two)]
    slice x18, local copies, waits for them, and re-layouts: 6.43 us -> 2.34 us  [window(): return jnp.roll(differences, 2 - offset, axis=along)]
    unnamed x72 -> x38, local copies, waits for them, and re-layouts: 5.93 us -> 2.83 us
    add x2 -> x6, other arithmetic: 55.2 us -> 56.8 us  [the longest x3 40.1 us: local_part(): partial + 0.5 * (alpha_three * (fore_three - back_three) + alpha_four * (...]
  transfers between devices with their start and end apart: 12 -> 18, of which waited for: 2 -> 7; matrix products, arithmetic and copies ran while one was open for 16% -> 26% of each run, Pallas kernels for 0% -> 0%
where the time goes in v1:
time: 239 us; the launch traced here: 238 us
  other arithmetic  114 us (48%)
  waiting for transfers between devices  56.6 us (24%)
  starting transfers between devices  46.4 us (19%)
  local copies, waits for them, and re-layouts  16.5 us (7%)
  between operations  4.59 us (2%)
    add x3, other arithmetic, local_part(): partial + 0.5 * (alpha_three * (fore_three - back_three) + alpha_four * (...  40.1 us
    ppermute x6, starting transfers between devices, exchange(): lax.ppermute(tail, axis, [(i, (i + 1) % count) for i in range(ends)])  28.4 us
    ppermute x6, waiting for transfers between devices, exchange(): lax.ppermute(tail, axis, [(i, (i + 1) % count) for i in range(ends)])  24.4 us
    ppermute x6, waiting for transfers between devices, exchange(): lax.ppermute(head, axis, [((i + 1) % count, i) for i in range(ends)])  20 us
    add x1, other arithmetic, on_device(): values * (1.0 / 3.0)  14 us
    add x1, other arithmetic, on_device(): second = 0.75 * values + 0.25 * (first + step_time * section_rate(first))  13.3 us
    ppermute x6, waiting for transfers between devices, spread_max(): lax.ppermute(local, axes, [(i, (i + k * span) % count) for i in range(cou...  12.2 us
    ppermute x6, starting transfers between devices, spread_max(): lax.ppermute(local, axes, [(i, (i + k * span) % count) for i in range(cou...  10.3 us
  transfers between devices with their start and end apart: 18, of which 7 were waited for; matrix products, arithmetic and copies ran while one was open for 26% of the time, Pallas kernels for 0%

profile of v1, /device:TPU:0, one launch (start us, length us, event | category | flops | bytes accessed | tf_op | source)
XLA Modules:
  0.0 238.0 jit_solution(11480761873386086291)
XLA Ops:
  0.0 1.4 fusion.54
  1.4 1.2 sine_multiply_fusion
  2.6 1.4 fusion.27
  3.9 1.2 abs_multiply_fusion
  5.1 1.1 abs_multiply_fusion.1
  6.2 0.8 fusion.52
  7.0 1.3 add_reduce_fusion.1
  8.3 2.0 add_reduce_fusion.2
  10.3 2.0 add_reduce_fusion.3
  12.3 1.9 pad_maximum_fusion.30
  14.2 2.4 %collective-permute-start.2 = (f32[2]{0:T(128)}, f32[2]{0:T(128)}, u32[]{:S(2)}, u32[]{:S(2)}) collective-permute-start(f32[2]{0:T(128)} %pad_maximum_fusion.30), channel_id=1, source_target_pairs={{0,3},{1,4},{2,5},{3,6},{4,7},{5,8},{6,9},{7,10},{8,11},{9,12},{10... | collective-permute-start | bytes 32 | tf_op jit(solution)/shard_map/ppermute | solution.py:187
  16.6 1.5 collective-permute-start.1
  18.2 0.5 collective-permute-start
  18.6 2.4 %fusion.51 = (f32[3,6,64,128]{3,2,1,0:T(8,128)}, f32[3,6,64,128]{3,2,1,0:T(8,128)}) fusion(f32[6,6,64,128]{3,2,1,0:T(8,128)} %param.3), kind=kLoop, calls=%fused_computation.185 | loop fusion | bytes 2359296 | tf_op jit(solution)/shard_map/slice | solution.py:168
  21.0 1.1 fusion.50
  22.2 1.3 collective-permute-start.9
  23.4 4.8 %collective-permute-start.8 = (f32[6,3,64,128]{3,2,1,0:T(8,128)}, f32[6,3,64,128]{3,2,1,0:T(8,128)}, u32[]{:S(2)}, u32[]{:S(2)}) collective-permute-start(f32[6,3,64,128]{3,2,1,0:T(8,128)} %get-tuple-element.32), channel_id=1, source_target_pairs={{0,1},{2,3},{4,5},{6,7},{8,9},{10,11},{12,13},{14,15},{16,17},{18,... | collective-permute-start | bytes 1769480 | tf_op jit(solution)/shard_map/ppermute | solution.py:175
  28.6 1.4 fusion.49
  30.0 1.4 slice.714
  31.5 2.1 slice_maximum_fusion.5
  33.6 1.4 slice_maximum_fusion.4
  38.0 0.9 slice_bitcast_fusion.9
  38.9 0.9 slice_bitcast_fusion.11
  39.8 0.6 copy-done.3
  40.5 0.4 copy-done.2
  40.9 13.8 %multiply_add_fusion.3 = (f32[6,6,64,128]{3,2,1,0:T(8,128)}, f32[6,6,64,128]{3,2,1,0:T(8,128)S(1)}, f32[6,6,64,128]{3,2,1,0:T(8,128)S(1)}) fusion(f32[6,6,64,1]{3,2,1,0:T(8,128)S(1)} %copy-done.4, f32[6,6,64,125]{3,2,1,0:T(8,128)S(1)} %copy-done.3, f32[6,6,64,126]{3,2,1,0:T(8,128)S(1)} %copy-done.6, f32[6,6,64,127]{3,2,1,0:T(8,128)S(1)} %subtract_multiply_fusion.2, ...), kind=kLoop, calls=%fused_computation.90 | loop fusion | flops 82575360 | bytes 16450572 | tf_op jit(solution)/shard_map/add | solution.py:244
  56.0 1.3 collective-permute-start.7
  57.3 5.4 %collective-permute-start.6 = (f32[3,6,64,128]{3,2,1,0:T(8,128)}, f32[3,6,64,128]{3,2,1,0:T(8,128)}, u32[]{:S(2)}, u32[]{:S(2)}) collective-permute-start(f32[3,6,64,128]{3,2,1,0:T(8,128)} %get-tuple-element.30), channel_id=1, source_target_pairs={{0,2},{2,4},{4,6},{6,8},{8,10},{10,12},{12,14},{1,3},{3,5},{5,7},{... | collective-permute-start | bytes 1769480 | tf_op jit(solution)/shard_map/ppermute | solution.py:175
  62.7 2.0 maximum_maximum_fusion.7
  64.7 2.2 collective-permute-start.5
  66.9 6.0 %collective-permute-done.5 = f32[2]{0:T(128)S(1)} collective-permute-done((f32[2]{0:T(128)S(1)}, f32[2]{0:T(128)S(1)}, u32[]{:S(2)}, u32[]{:S(2)}) %collective-permute-start.5) | collective-permute-done | bytes 40 | tf_op jit(solution)/shard_map/ppermute | solution.py:187
  72.9 2.1 collective-permute-start.4
  75.0 2.4 %collective-permute-done.4 = f32[2]{0:T(128)S(1)} collective-permute-done((f32[2]{0:T(128)S(1)}, f32[2]{0:T(128)S(1)}, u32[]{:S(2)}, u32[]{:S(2)}) %collective-permute-start.4) | collective-permute-done | bytes 40 | tf_op jit(solution)/shard_map/ppermute | solution.py:187
  77.4 1.6 collective-permute-start.3
  78.9 3.8 %collective-permute-done.3 = f32[2]{0:T(128)S(1)} collective-permute-done((f32[2]{0:T(128)S(1)}, f32[2]{0:T(128)S(1)}, u32[]{:S(2)}, u32[]{:S(2)}) %collective-permute-start.3) | collective-permute-done | bytes 40 | tf_op jit(solution)/shard_map/ppermute | solution.py:187
  82.7 0.6 fusion.53
  84.8 1.2 add_select_fusion.8
  86.4 0.7 copy-done.9
  87.2 1.2 add_select_fusion.10
  88.9 0.5 copy-done.7
  90.1 10.2 %fusion.29 = (f32[6,6,64,128]{3,2,1,0:T(8,128)S(1)}, f32[6,6,64,128]{3,2,1,0:T(8,128)S(1)}, f32[6,6,64,128]{3,2,1,0:T(8,128)S(1)}, f32[6,6,64,128]{3,2,1,0:T(8,1...) fusion(f32[6,11,64,128]{3,2,1,0:T(8,128)S(1)} %fusion.4, f32[11,6,64,128]{3,2,1,0:T(8,128)S(1)} %fusion.5), kind=kLoop, calls=%fused_computation.163 | loop fusion | flops 73728000 | bytes 21233664 | tf_op jit(solution)/shard_map/sub | solution.py:261
  100.3 1.6 fusion.8
  101.9 1.8 multiply_add_fusion.2
  104.4 0.4 fusion.42
  105.2 0.7 slice_maximum_fusion.3
  106.3 0.5 broadcast_multiply_fusion.1
  107.6 1.3 collective-permute-start.13
  108.9 3.1 %collective-permute-start.12 = (f32[6,3,64,128]{3,2,1,0:T(8,128)S(1)}, f32[6,3,64,128]{3,2,1,0:T(8,128)S(1)}, u32[]{:S(2)}, u32[]{:S(2)}) collective-permute-start(f32[6,3,64,128]{3,2,1,0:T(8,128)S(1)} %get-tuple-element.42), channel_id=1, source_target_pairs={{0,1},{2,3},{4,5},{6,7},{8,9},{10,11},{12,13},{14,15},{16,17},{18,... | collective-permute-start | bytes 1769480 | tf_op jit(solution)/shard_map/ppermute | solution.py:175
  112.0 13.1 %multiply_add_fusion.1 = (f32[6,6,64,128]{3,2,1,0:T(8,128)S(1)}, f32[6,6,64,128]{3,2,1,0:T(8,128)S(1)}, f32[6,6,64,128]{3,2,1,0:T(8,128)S(1)}) fusion(f32[6,6,64,1]{3,2,1,0:T(8,128)S(1)} %get-tuple-element.119, f32[6,6,64,125]{3,2,1,0:T(8,128)S(1)} %slice.752, f32[6,6,64,126]{3,2,1,0:T(8,128)S(1)} %get-tuple-element.117, ...), kind=kLoop, calls=%fused_computation.84 | loop fusion | flops 82575360 | bytes 16450572 | tf_op jit(solution)/shard_map/add | solution.py:244
  125.5 1.3 collective-permute-start.11
  126.8 7.0 %collective-permute-start.10 = (f32[3,6,64,128]{3,2,1,0:T(8,128)S(1)}, f32[3,6,64,128]{3,2,1,0:T(8,128)S(1)}, u32[]{:S(2)}, u32[]{:S(2)}) collective-permute-start(f32[3,6,64,128]{3,2,1,0:T(8,128)S(1)} %get-tuple-element.40), channel_id=1, source_target_pairs={{0,2},{2,4},{4,6},{6,8},{8,10},{10,12},{12,14},{1,3},{3,5},{5,7},{... | collective-permute-start | bytes 1769480 | tf_op jit(solution)/shard_map/ppermute | solution.py:175
  134.5 9.9 %collective-permute-done.11 = f32[3,6,64,128]{3,2,1,0:T(8,128)S(1)} collective-permute-done((f32[3,6,64,128]{3,2,1,0:T(8,128)S(1)}, f32[3,6,64,128]{3,2,1,0:T(8,128)S(1)}, u32[]{:S(2)}, u32[]{:S(2)}) %collective-permute-start.11) | collective-permute-done | bytes 589856 | tf_op jit(solution)/shard_map/ppermute | solution.py:176
  145.0 12.2 %collective-permute-done.10 = f32[3,6,64,128]{3,2,1,0:T(8,128)S(1)} collective-permute-done((f32[3,6,64,128]{3,2,1,0:T(8,128)S(1)}, f32[3,6,64,128]{3,2,1,0:T(8,128)S(1)}, u32[]{:S(2)}, u32[]{:S(2)}) %collective-permute-start.10) | collective-permute-done | bytes 589856 | tf_op jit(solution)/shard_map/ppermute | solution.py:175
  158.1 13.3 %fusion.16 = f32[6,6,64,128]{3,2,1,0:T(8,128)S(1)} fusion(f32[6,6,64,128]{3,2,1,0:T(8,128)S(1)} %multiply_add_fusion.2, f32[6,6,64,128]{3,2,1,0:T(8,128)S(1)} %get-tuple-element.45, f32[6,6,64,128]{3,2,1,0:T(8,128)S(1)} %add_multiply_fusion.4, f32[6,11,64,128]{3,2,1,0:T(8,128)S(1)} %fusion.2, f32[11,6,64,128]{3,2,1,0:T(8,128)S(1)} %fusion.3, ...), kind=kLoop, calls=%fused_computation.31 | loop fusion | flops 81100800 | bytes 20096208 | tf_op jit(solution)/shard_map/add | solution.py:271
  172.8 0.7 slice_maximum_fusion.1
  173.9 0.5 broadcast_multiply_fusion
  175.2 1.3 collective-permute-start.17
  176.5 3.1 %collective-permute-start.16 = (f32[6,3,64,128]{3,2,1,0:T(8,128)S(1)}, f32[6,3,64,128]{3,2,1,0:T(8,128)S(1)}, u32[]{:S(2)}, u32[]{:S(2)}) collective-permute-start(f32[6,3,64,128]{3,2,1,0:T(8,128)S(1)} %get-tuple-element.49), channel_id=1, source_target_pairs={{0,1},{2,3},{4,5},{6,7},{8,9},{10,11},{12,13},{14,15},{16,17},{18,... | collective-permute-start | bytes 1769480 | tf_op jit(solution)/shard_map/ppermute | solution.py:175
  179.6 13.1 %multiply_add_fusion = (f32[6,6,64,128]{3,2,1,0:T(8,128)S(1)}, f32[6,6,64,128]{3,2,1,0:T(8,128)S(1)}, f32[6,6,64,128]{3,2,1,0:T(8,128)S(1)}) fusion(f32[6,6,64,1]{3,2,1,0:T(8,128)S(1)} %get-tuple-element.95, f32[6,6,64,125]{3,2,1,0:T(8,128)S(1)} %slice.790, f32[6,6,64,126]{3,2,1,0:T(8,128)S(1)} %get-tuple-element.93, ...), kind=kLoop, calls=%fused_computation.79 | loop fusion | flops 82575360 | bytes 16450572 | tf_op jit(solution)/shard_map/add | solution.py:244
  193.1 1.3 collective-permute-start.15
  194.4 5.1 %collective-permute-start.14 = (f32[3,6,64,128]{3,2,1,0:T(8,128)S(1)}, f32[3,6,64,128]{3,2,1,0:T(8,128)S(1)}, u32[]{:S(2)}, u32[]{:S(2)}) collective-permute-start(f32[3,6,64,128]{3,2,1,0:T(8,128)S(1)} %get-tuple-element.47), channel_id=1, source_target_pairs={{0,2},{2,4},{4,6},{6,8},{8,10},{10,12},{12,14},{1,3},{3,5},{5,7},{... | collective-permute-start | bytes 1769480 | tf_op jit(solution)/shard_map/ppermute | solution.py:175
  200.2 10.1 %collective-permute-done.15 = f32[3,6,64,128]{3,2,1,0:T(8,128)S(1)} collective-permute-done((f32[3,6,64,128]{3,2,1,0:T(8,128)S(1)}, f32[3,6,64,128]{3,2,1,0:T(8,128)S(1)}, u32[]{:S(2)}, u32[]{:S(2)}) %collective-permute-start.15) | collective-permute-done | bytes 589856 | tf_op jit(solution)/shard_map/ppermute | solution.py:176
  210.9 12.2 %collective-permute-done.14 = f32[3,6,64,128]{3,2,1,0:T(8,128)S(1)} collective-permute-done((f32[3,6,64,128]{3,2,1,0:T(8,128)S(1)}, f32[3,6,64,128]{3,2,1,0:T(8,128)S(1)}, u32[]{:S(2)}, u32[]{:S(2)}) %collective-permute-start.14) | collective-permute-done | bytes 589856 | tf_op jit(solution)/shard_map/ppermute | solution.py:175
  224.0 14.0 %fusion.24 = f32[6,6,64,128]{3,2,1,0:T(8,128)} fusion(f32[6,6,64,128]{3,2,1,0:T(8,128)S(1)} %fusion.16, f32[6,6,64,128]{3,2,1,0:T(8,128)S(1)} %get-tuple-element.52, f32[6,6,64,128]{3,2,1,0:T(8,128)S(1)} %add_multiply_fusion.3, f32[6,11,64,128]{3,2,1,0:T(8,128)S(1)} %fusion, f32[11,6,64,128]{3,2,1,0:T(8,128)S(1)} %fusion.1, ...), kind=kLoop, calls=%fused_computation.39 | loop fusion | flops 81100800 | bytes 20096208 | tf_op jit(solution)/shard_map/add | solution.py:272
  (114 shorter events, 13.4 us)
Async XLA Ops:
  14.2 6.8 %copy-start = (f32[6,6,64,128]{3,2,1,0:T(8,128)S(1)}, f32[6,6,64,128]{3,2,1,0:T(8,128)}, u32[]{:S(2)}) copy-start(f32[6,6,64,128]{3,2,1,0:T(8,128)} %param.3) | copy-start | bytes 3538948
  14.2 41.8 %collective-permute-start.2 = (f32[2]{0:T(128)}, f32[2]{0:T(128)}, u32[]{:S(2)}, u32[]{:S(2)}) collective-permute-start(f32[2]{0:T(128)} %pad_maximum_fusion.30), channel_id=1, source_target_pairs={{0,3},{1,4},{2,5},{3,6},{4,7},{5,8},{6,9},{7,10},{8,11},{9,12},{10... | collective-permute-start | bytes 32 | tf_op jit(solution)/shard_map/ppermute | solution.py:187
  16.6 40.6 %collective-permute-start.1 = (f32[2]{0:T(128)}, f32[2]{0:T(128)}, u32[]{:S(2)}, u32[]{:S(2)}) collective-permute-start(f32[2]{0:T(128)} %pad_maximum_fusion.30), channel_id=1, source_target_pairs={{0,2},{1,3},{2,4},{3,5},{4,6},{5,7},{6,8},{7,9},{8,10},{9,11},{10,... | collective-permute-start | bytes 32 | tf_op jit(solution)/shard_map/ppermute | solution.py:187
  18.2 44.5 %collective-permute-start = (f32[2]{0:T(128)}, f32[2]{0:T(128)}, u32[]{:S(2)}, u32[]{:S(2)}) collective-permute-start(f32[2]{0:T(128)} %pad_maximum_fusion.30), channel_id=1, source_target_pairs={{0,1},{1,2},{2,3},{3,4},{4,5},{5,6},{6,7},{7,8},{8,9},{9,10},{10,1... | collective-permute-start | bytes 32 | tf_op jit(solution)/shard_map/ppermute | solution.py:187
  22.2 62.6 %collective-permute-start.9 = (f32[6,3,64,128]{3,2,1,0:T(8,128)}, f32[6,3,64,128]{3,2,1,0:T(8,128)}, u32[]{:S(2)}, u32[]{:S(2)}) collective-permute-start(f32[6,3,64,128]{3,2,1,0:T(8,128)} %get-tuple-element.33), channel_id=1, source_target_pairs={{1,0},{3,2},{5,4},{7,6},{9,8},{11,10},{13,12},{15,14},{17,16},{19,... | collective-permute-start | bytes 1769480 | tf_op jit(solution)/shard_map/ppermute | solution.py:176
  23.4 62.5 %collective-permute-start.8 = (f32[6,3,64,128]{3,2,1,0:T(8,128)}, f32[6,3,64,128]{3,2,1,0:T(8,128)}, u32[]{:S(2)}, u32[]{:S(2)}) collective-permute-start(f32[6,3,64,128]{3,2,1,0:T(8,128)} %get-tuple-element.32), channel_id=1, source_target_pairs={{0,1},{2,3},{4,5},{6,7},{8,9},{10,11},{12,13},{14,15},{16,17},{18,... | collective-permute-start | bytes 1769480 | tf_op jit(solution)/shard_map/ppermute | solution.py:175
  37.5 2.3 copy-start.6
  37.8 2.0 copy-start.4
  37.8 2.0 copy-start.5
  38.0 2.5 %copy-start.3 = (f32[6,6,64,125]{3,2,1,0:T(8,128)S(1)}, f32[6,6,64,125]{3,2,1,0:T(8,128)}, u32[]{:S(2)}) copy-start(f32[6,6,64,125]{3,2,1,0:T(8,128)} %slice.714) | copy-start | bytes 3456004
  38.9 2.0 copy-start.2
  54.8 0.6 copy-start.18
  54.8 30.0 %copy-start.13 = (f32[6,64,128]{2,1,0:T(8,128)S(1)}, f32[6,64,128]{2,1,0:T(8,128)}, u32[]{:S(2)}) copy-start(f32[6,64,128]{2,1,0:T(8,128)} %get-tuple-element.129) | copy-start | bytes 589828
  54.8 30.0 %copy-start.14 = (f32[6,64,128]{2,1,0:T(8,128)S(1)}, f32[6,64,128]{2,1,0:T(8,128)}, u32[]{:S(2)}) copy-start(f32[6,64,128]{2,1,0:T(8,128)} %get-tuple-element.130) | copy-start | bytes 589828
  54.9 31.0 %copy-start.11 = (f32[6,64,128]{2,1,0:T(8,128)S(1)}, f32[6,64,128]{2,1,0:T(8,128)}, u32[]{:S(2)}) copy-start(f32[6,64,128]{2,1,0:T(8,128)} %get-tuple-element.128) | copy-start | bytes 589828
  55.0 31.0 %copy-start.12 = (f32[6,64,128]{2,1,0:T(8,128)S(1)}, f32[6,64,128]{2,1,0:T(8,128)}, u32[]{:S(2)}) copy-start(f32[6,64,128]{2,1,0:T(8,128)} %get-tuple-element.131) | copy-start | bytes 589828
  56.0 30.4 %collective-permute-start.7 = (f32[3,6,64,128]{3,2,1,0:T(8,128)}, f32[3,6,64,128]{3,2,1,0:T(8,128)}, u32[]{:S(2)}, u32[]{:S(2)}) collective-permute-start(f32[3,6,64,128]{3,2,1,0:T(8,128)} %get-tuple-element.31), channel_id=1, source_target_pairs={{2,0},{4,2},{6,4},{8,6},{10,8},{12,10},{14,12},{3,1},{5,3},{7,5},{... | collective-permute-start | bytes 1769480 | tf_op jit(solution)/shard_map/ppermute | solution.py:176
  57.3 31.6 %collective-permute-start.6 = (f32[3,6,64,128]{3,2,1,0:T(8,128)}, f32[3,6,64,128]{3,2,1,0:T(8,128)}, u32[]{:S(2)}, u32[]{:S(2)}) collective-permute-start(f32[3,6,64,128]{3,2,1,0:T(8,128)} %get-tuple-element.30), channel_id=1, source_target_pairs={{0,2},{2,4},{4,6},{6,8},{8,10},{10,12},{12,14},{1,3},{3,5},{5,7},{... | collective-permute-start | bytes 1769480 | tf_op jit(solution)/shard_map/ppermute | solution.py:175
  64.7 8.2 %collective-permute-start.5 = (f32[2]{0:T(128)S(1)}, f32[2]{0:T(128)S(1)}, u32[]{:S(2)}, u32[]{:S(2)}) collective-permute-start(f32[2]{0:T(128)S(1)} %maximum_maximum_fusion.7), channel_id=1, source_target_pairs={{0,12},{1,13},{2,14},{3,15},{4,0},{5,1},{6,2},{7,3},{8,4},{9,5},{1... | collective-permute-start | bytes 32 | tf_op jit(solution)/shard_map/ppermute | solution.py:187
  72.9 4.5 %collective-permute-start.4 = (f32[2]{0:T(128)S(1)}, f32[2]{0:T(128)S(1)}, u32[]{:S(2)}, u32[]{:S(2)}) collective-permute-start(f32[2]{0:T(128)S(1)} %maximum_maximum_fusion.7), channel_id=1, source_target_pairs={{0,8},{1,9},{2,10},{3,11},{4,12},{5,13},{6,14},{7,15},{8,0},{9,1},... | collective-permute-start | bytes 32 | tf_op jit(solution)/shard_map/ppermute | solution.py:187
  77.4 5.4 %collective-permute-start.3 = (f32[2]{0:T(128)S(1)}, f32[2]{0:T(128)S(1)}, u32[]{:S(2)}, u32[]{:S(2)}) collective-permute-start(f32[2]{0:T(128)S(1)} %maximum_maximum_fusion.7), channel_id=1, source_target_pairs={{0,4},{1,5},{2,6},{3,7},{4,8},{5,9},{6,10},{7,11},{8,12},{9,13},{1... | collective-permute-start | bytes 32 | tf_op jit(solution)/shard_map/ppermute | solution.py:187
  86.2 0.9 copy-start.9
  86.2 1.0 copy-start.10
  88.4 0.9 copy-start.7
  88.4 1.0 copy-start.8
  90.1 10.2 %copy-start.1 = (f32[6,6,64,128]{3,2,1,0:T(8,128)S(1)}, f32[6,6,64,128]{3,2,1,0:T(8,128)}, u32[]{:S(2)}) copy-start(f32[6,6,64,128]{3,2,1,0:T(8,128)} %get-tuple-element.35) | copy-start | bytes 3538948
  90.1 10.2 %copy-start.15 = (f32[64,128]{1,0:T(8,128)S(1)}, f32[64,128]{1,0:T(8,128)}, u32[]{:S(2)}) copy-start(f32[64,128]{1,0:T(8,128)} %get-tuple-element.150) | copy-start | bytes 98308
  90.1 10.2 %copy-start.16 = (f32[6]{0:T(128)S(1)}, f32[6]{0:T(128)}, u32[]{:S(2)}) copy-start(f32[6]{0:T(128)} %get-tuple-element.158) | copy-start | bytes 76
  90.1 10.2 %copy-start.17 = (f32[6]{0:T(128)S(1)}, f32[6]{0:T(128)}, u32[]{:S(2)}) copy-start(f32[6]{0:T(128)} %get-tuple-element.166) | copy-start | bytes 76
  107.6 26.2 %collective-permute-start.13 = (f32[6,3,64,128]{3,2,1,0:T(8,128)S(1)}, f32[6,3,64,128]{3,2,1,0:T(8,128)S(1)}, u32[]{:S(2)}, u32[]{:S(2)}) collective-permute-start(f32[6,3,64,128]{3,2,1,0:T(8,128)S(1)} %get-tuple-element.43), channel_id=1, source_target_pairs={{1,0},{3,2},{5,4},{7,6},{9,8},{11,10},{13,12},{15,14},{17,16},{19,... | collective-permute-start | bytes 1769480 | tf_op jit(solution)/shard_map/ppermute | solution.py:176
  108.9 25.1 %collective-permute-start.12 = (f32[6,3,64,128]{3,2,1,0:T(8,128)S(1)}, f32[6,3,64,128]{3,2,1,0:T(8,128)S(1)}, u32[]{:S(2)}, u32[]{:S(2)}) collective-permute-start(f32[6,3,64,128]{3,2,1,0:T(8,128)S(1)} %get-tuple-element.42), channel_id=1, source_target_pairs={{0,1},{2,3},{4,5},{6,7},{8,9},{10,11},{12,13},{14,15},{16,17},{18,... | collective-permute-start | bytes 1769480 | tf_op jit(solution)/shard_map/ppermute | solution.py:175
  125.5 18.9 %collective-permute-start.11 = (f32[3,6,64,128]{3,2,1,0:T(8,128)S(1)}, f32[3,6,64,128]{3,2,1,0:T(8,128)S(1)}, u32[]{:S(2)}, u32[]{:S(2)}) collective-permute-start(f32[3,6,64,128]{3,2,1,0:T(8,128)S(1)} %get-tuple-element.41), channel_id=1, source_target_pairs={{2,0},{4,2},{6,4},{8,6},{10,8},{12,10},{14,12},{3,1},{5,3},{7,5},{... | collective-permute-start | bytes 1769480 | tf_op jit(solution)/shard_map/ppermute | solution.py:176
  126.8 30.4 %collective-permute-start.10 = (f32[3,6,64,128]{3,2,1,0:T(8,128)S(1)}, f32[3,6,64,128]{3,2,1,0:T(8,128)S(1)}, u32[]{:S(2)}, u32[]{:S(2)}) collective-permute-start(f32[3,6,64,128]{3,2,1,0:T(8,128)S(1)} %get-tuple-element.40), channel_id=1, source_target_pairs={{0,2},{2,4},{4,6},{6,8},{8,10},{10,12},{12,14},{1,3},{3,5},{5,7},{... | collective-permute-start | bytes 1769480 | tf_op jit(solution)/shard_map/ppermute | solution.py:175
  175.2 24.3 %collective-permute-start.17 = (f32[6,3,64,128]{3,2,1,0:T(8,128)S(1)}, f32[6,3,64,128]{3,2,1,0:T(8,128)S(1)}, u32[]{:S(2)}, u32[]{:S(2)}) collective-permute-start(f32[6,3,64,128]{3,2,1,0:T(8,128)S(1)} %get-tuple-element.50), channel_id=1, source_target_pairs={{1,0},{3,2},{5,4},{7,6},{9,8},{11,10},{13,12},{15,14},{17,16},{19,... | collective-permute-start | bytes 1769480 | tf_op jit(solution)/shard_map/ppermute | solution.py:176
  176.5 23.2 %collective-permute-start.16 = (f32[6,3,64,128]{3,2,1,0:T(8,128)S(1)}, f32[6,3,64,128]{3,2,1,0:T(8,128)S(1)}, u32[]{:S(2)}, u32[]{:S(2)}) collective-permute-start(f32[6,3,64,128]{3,2,1,0:T(8,128)S(1)} %get-tuple-element.49), channel_id=1, source_target_pairs={{0,1},{2,3},{4,5},{6,7},{8,9},{10,11},{12,13},{14,15},{16,17},{18,... | collective-permute-start | bytes 1769480 | tf_op jit(solution)/shard_map/ppermute | solution.py:175
  193.1 17.2 %collective-permute-start.15 = (f32[3,6,64,128]{3,2,1,0:T(8,128)S(1)}, f32[3,6,64,128]{3,2,1,0:T(8,128)S(1)}, u32[]{:S(2)}, u32[]{:S(2)}) collective-permute-start(f32[3,6,64,128]{3,2,1,0:T(8,128)S(1)} %get-tuple-element.48), channel_id=1, source_target_pairs={{2,0},{4,2},{6,4},{8,6},{10,8},{12,10},{14,12},{3,1},{5,3},{7,5},{... | collective-permute-start | bytes 1769480 | tf_op jit(solution)/shard_map/ppermute | solution.py:176
  194.4 28.7 %collective-permute-start.14 = (f32[3,6,64,128]{3,2,1,0:T(8,128)S(1)}, f32[3,6,64,128]{3,2,1,0:T(8,128)S(1)}, u32[]{:S(2)}, u32[]{:S(2)}) collective-permute-start(f32[3,6,64,128]{3,2,1,0:T(8,128)S(1)} %get-tuple-element.47), channel_id=1, source_target_pairs={{0,2},{2,4},{4,6},{6,8},{8,10},{10,12},{12,14},{1,3},{3,5},{5,7},{... | collective-permute-start | bytes 1769480 | tf_op jit(solution)/shard_map/ppermute | solution.py:175
